TPU v7x, 32 devices: a whole 2x2x4 slice. The times are simulated.
32 devices in a mesh: dp: 8 (over y, x, core), tensor: 4 (over z).
Axes of the slice: x: 2, y: 2, z: 4, core: 2. Of those that a mesh axis runs over, the one named last changes fastest.
Arguments:
- tokens: bfloat16 [8, 2048, 1024], P('dp', 'tensor'), may hold values from -6 to 6
- seg_ids: int32 [8, 2048], P('dp'), may hold values from 0 to 146, never falling along the last dimension, each value on 1 to 15 neighbouring positions
- norm1_gain: float32 [1024], replicated, may hold values from 0.25 to 1.75
- norm1_bias: float32 [1024], replicated, may hold values from -2 to 2
- w_qkv: bfloat16 [1024, 3, 1024], P(None, None, 'tensor'), may hold values from -0.1875 to 0.1875
- w_out: bfloat16 [1024, 1024], P('tensor'), may hold values from -0.5 to 0.5
- norm2_gain: float32 [1024], replicated, may hold values from 0.25 to 1.75
- norm2_bias: float32 [1024], replicated, may hold values from -2 to 2
- w_in: bfloat16 [1024, 2048], P(None, 'tensor'), may hold values from -0.1875 to 0.1875
- w_down: bfloat16 [2048, 1024], P('tensor'), may hold values from -0.125 to 0.125
- cotangent: bfloat16 [8, 2048, 1024], P('dp', 'tensor'), may hold values from -6 to 6
Outputs:
- out_act: bfloat16 [8, 2048, 1024], P('dp', 'tensor')
- grad_tokens: float32 [8, 2048, 1024], P('dp', 'tensor')
- grad_norm1_gain: float32 [1024], replicated
- grad_norm1_bias: float32 [1024], replicated
- grad_qkv: float32 [1024, 3, 1024], P(None, None, 'tensor')
- grad_wout: float32 [1024, 1024], P('tensor')
- grad_norm2_gain: float32 [1024], replicated
- grad_norm2_bias: float32 [1024], replicated
- grad_win: float32 [1024, 2048], P(None, 'tensor')
- grad_wdown: float32 [2048, 1024], P('tensor')
Inputs may be any that keep to these rules, and one draw needn't show every extreme that they name: `seg_ids`: within each pack the context numbers never fall, start at 0 and take every value up to 146; each context holds 1 to 15 tokens and one holds exactly 15.
All inputs are finite; a program needn't handle non-finite values.
Results may differ from a plain program's by a relative error of at most 0.019.
Values may be sent and summed in bfloat16 or wider, within the bound.
No kernel may reach another device: no remote copies, remote signals or barrier semaphores. Data moves between devices by JAX's collectives and lax.ppermute only.
A program may use at most 128 MiB of HBM per device.

v0:
```python
from functools import partial

import jax
import jax.numpy as jnp
from jax import lax
from jax.sharding import PartitionSpec as P

HEAD_DIM = 128


eps_norm = 1e-05
key_margin = 128
block_limit = 512


def norm_forward(values, gain, bias):
    center = values - jnp.mean(values, axis=-1, keepdims=True)
    spread = jnp.mean(center * center, axis=-1, keepdims=True)
    scaled = lax.rsqrt(spread + eps_norm)
    normal = center * scaled
    return (normal * gain + bias, normal, scaled)


def norm_backward(upstream, normal, scaled, gain):
    weighted = upstream * gain
    inner = (
        weighted
        - jnp.mean(weighted, axis=-1, keepdims=True)
        - normal * jnp.mean(weighted * normal, axis=-1, keepdims=True)
    )
    return (scaled * inner, jnp.sum(upstream * normal, axis=0), jnp.sum(upstream, axis=0))


def block_view(array, start, count, heads_here):
    return lax.dynamic_slice_in_dim(array, start, count, 0).reshape(count, heads_here, HEAD_DIM)


def block_mask(seg_pad, start, block):
    query_segs = lax.dynamic_slice_in_dim(seg_pad, start + key_margin, block, 0)
    key_segs = lax.dynamic_slice_in_dim(seg_pad, start, block + key_margin, 0)
    query_place = jnp.arange(block)[:, None] + key_margin
    key_place = jnp.arange(block + key_margin)[None, :]
    return (query_segs[:, None] == key_segs[None, :]) & (key_place <= query_place)


def block_scores(query_blk, key_blk, allowed, scale):
    raw = jnp.einsum("qhd,khd->hqk", query_blk, key_blk, preferred_element_type=jnp.float32)
    return jnp.where(allowed[None], raw * scale, -1e30)


def local(
    tokens,
    seg_ids,
    norm1_gain,
    norm1_bias,
    w_qkv,
    w_out,
    norm2_gain,
    norm2_bias,
    w_in,
    w_down,
    cotangent,
):
    rows = tokens[0].astype(jnp.float32)
    width = rows.shape[1]
    local_cols = w_qkv.shape[2]
    heads_here = local_cols // HEAD_DIM
    scale = HEAD_DIM ** (-0.5)
    total = seg_ids.shape[1]
    block = min(block_limit, total)
    nblocks = total // block
    seg_pad = jnp.concatenate([jnp.full((key_margin,), -1, jnp.int32), seg_ids[0]])
    weight_qkv = w_qkv.reshape(width, 3 * local_cols)
    normed1, normal1, rstd1 = norm_forward(rows, norm1_gain, norm1_bias)
    full1 = lax.all_gather(normed1.astype(jnp.bfloat16), "tensor", axis=0, tiled=True)
    packed = jnp.dot(full1, weight_qkv, preferred_element_type=jnp.float32)
    queries = packed[:, :local_cols].astype(jnp.bfloat16)
    front = jnp.zeros((key_margin, 2 * local_cols), jnp.bfloat16)
    keyvals = jnp.concatenate([front, packed[:, local_cols:].astype(jnp.bfloat16)], axis=0)
    keys_pad = keyvals[:, :local_cols]
    values_pad = keyvals[:, local_cols:]

    def attend(start):
        query_blk = block_view(queries, start, block, heads_here)
        key_blk = block_view(keys_pad, start, block + key_margin, heads_here)
        value_blk = block_view(values_pad, start, block + key_margin, heads_here)
        masked = block_scores(query_blk, key_blk, block_mask(seg_pad, start, block), scale)
        top = jnp.max(masked, axis=-1, keepdims=True)
        expo = jnp.exp(masked - top)
        mass = jnp.sum(expo, axis=-1, keepdims=True)
        probs = expo / mass
        result = jnp.einsum(
            "hqk,khd->qhd",
            probs.astype(jnp.bfloat16),
            value_blk,
            preferred_element_type=jnp.float32,
        )
        return (
            result.astype(jnp.bfloat16).reshape(block, local_cols),
            (top + jnp.log(mass))[..., 0],
        )

    blocks_out, log_mass = lax.map(attend, jnp.arange(nblocks) * block)
    attended = blocks_out.reshape(total, local_cols)
    mixed = rows + lax.psum_scatter(
        jnp.dot(attended, w_out, preferred_element_type=jnp.float32).astype(jnp.bfloat16),
        "tensor",
        scatter_dimension=0,
        tiled=True,
    ).astype(jnp.float32)
    normed2, normal2, rstd2 = norm_forward(mixed, norm2_gain, norm2_bias)
    full2 = lax.all_gather(normed2.astype(jnp.bfloat16), "tensor", axis=0, tiled=True)
    pre_act = jnp.dot(full2, w_in, preferred_element_type=jnp.float32)
    hidden = jax.nn.gelu(pre_act, approximate=False).astype(jnp.bfloat16)
    final = mixed + lax.psum_scatter(
        jnp.dot(hidden, w_down, preferred_element_type=jnp.float32).astype(jnp.bfloat16),
        "tensor",
        scatter_dimension=0,
        tiled=True,
    ).astype(jnp.float32)
    out_act = final.astype(jnp.bfloat16)[None]
    grad_final = cotangent[0].astype(jnp.float32)
    grad_full = lax.all_gather(cotangent[0], "tensor", axis=0, tiled=True)
    grad_wdown = jnp.einsum("tf,td->fd", hidden, grad_full, preferred_element_type=jnp.float32)
    grad_hidden = jnp.einsum("td,fd->tf", grad_full, w_down, preferred_element_type=jnp.float32)
    ignored, gelu_pull = jax.vjp(partial(jax.nn.gelu, approximate=False), pre_act)
    grad_pre = gelu_pull(grad_hidden)[0].astype(jnp.bfloat16)
    grad_win = jnp.einsum("td,tf->df", full2, grad_pre, preferred_element_type=jnp.float32)
    grad_normed2 = lax.psum_scatter(
        jnp.einsum("tf,df->td", grad_pre, w_in, preferred_element_type=jnp.float32).astype(
            jnp.bfloat16
        ),
        "tensor",
        scatter_dimension=0,
        tiled=True,
    ).astype(jnp.float32)
    grad_back2, grad_gain2, grad_bias2 = norm_backward(grad_normed2, normal2, rstd2, norm2_gain)
    grad_mixed = grad_final + grad_back2
    grad_mid_full = lax.all_gather(grad_mixed.astype(jnp.bfloat16), "tensor", axis=0, tiled=True)
    grad_wout = jnp.einsum("tc,td->cd", attended, grad_mid_full, preferred_element_type=jnp.float32)
    grad_att = jnp.einsum(
        "td,cd->tc", grad_mid_full, w_out, preferred_element_type=jnp.float32
    ).astype(jnp.bfloat16)

    def back_step(carry, index):
        grad_keys_pad, grad_values_pad = carry
        start = index * block
        query_blk = block_view(queries, start, block, heads_here)
        key_blk = block_view(keys_pad, start, block + key_margin, heads_here)
        value_blk = block_view(values_pad, start, block + key_margin, heads_here)
        masked = block_scores(query_blk, key_blk, block_mask(seg_pad, start, block), scale)
        probs = jnp.exp(masked - log_mass[index][:, :, None])
        grad_blk = block_view(grad_att, start, block, heads_here)
        value_part = jnp.einsum(
            "hqk,qhd->khd", probs.astype(jnp.bfloat16), grad_blk, preferred_element_type=jnp.float32
        )
        grad_prob = jnp.einsum(
            "qhd,khd->hqk", grad_blk, value_blk, preferred_element_type=jnp.float32
        )
        inner = jnp.sum(probs * grad_prob, axis=-1, keepdims=True)
        grad_raw = (probs * (grad_prob - inner) * scale).astype(jnp.bfloat16)
        query_part = jnp.einsum(
            "hqk,khd->qhd", grad_raw, key_blk, preferred_element_type=jnp.float32
        )
        key_part = jnp.einsum(
            "hqk,qhd->khd", grad_raw, query_blk, preferred_element_type=jnp.float32
        )
        span = block + key_margin
        grad_keys_pad = lax.dynamic_update_slice_in_dim(
            grad_keys_pad,
            lax.dynamic_slice_in_dim(grad_keys_pad, start, span, 0)
            + key_part.reshape(span, local_cols),
            start,
            0,
        )
        grad_values_pad = lax.dynamic_update_slice_in_dim(
            grad_values_pad,
            lax.dynamic_slice_in_dim(grad_values_pad, start, span, 0)
            + value_part.reshape(span, local_cols),
            start,
            0,
        )
        return ((grad_keys_pad, grad_values_pad), query_part.reshape(block, local_cols))

    empty = jnp.zeros((total + key_margin, local_cols), jnp.float32)
    (grad_keys_pad, grad_values_pad), grad_query_blocks = lax.scan(
        back_step, (empty, empty), jnp.arange(nblocks)
    )
    grad_proj = jnp.concatenate(
        [
            grad_query_blocks.reshape(total, local_cols),
            grad_keys_pad[key_margin:],
            grad_values_pad[key_margin:],
        ],
        axis=1,
    ).astype(jnp.bfloat16)
    grad_qkv = jnp.einsum(
        "td,tc->dc", full1, grad_proj, preferred_element_type=jnp.float32
    ).reshape(width, 3, local_cols)
    grad_normed1 = lax.psum_scatter(
        jnp.einsum("tc,dc->td", grad_proj, weight_qkv, preferred_element_type=jnp.float32).astype(
            jnp.bfloat16
        ),
        "tensor",
        scatter_dimension=0,
        tiled=True,
    ).astype(jnp.float32)
    grad_back1, grad_gain1, grad_bias1 = norm_backward(grad_normed1, normal1, rstd1, norm1_gain)
    grad_tokens = (grad_mixed + grad_back1)[None]
    grad_gain1, grad_bias1, grad_gain2, grad_bias2 = lax.psum(
        (grad_gain1, grad_bias1, grad_gain2, grad_bias2), ("dp", "tensor")
    )
    grad_qkv, grad_wout, grad_win, grad_wdown = lax.psum(
        (grad_qkv, grad_wout, grad_win, grad_wdown), "dp"
    )
    return (
        out_act,
        grad_tokens,
        grad_gain1,
        grad_bias1,
        grad_qkv,
        grad_wout,
        grad_gain2,
        grad_bias2,
        grad_win,
        grad_wdown,
    )


def solution(mesh):
    return jax.shard_map(
        local,
        mesh=mesh,
        in_specs=(
            P("dp", "tensor", None),
            P("dp", None),
            P(),
            P(),
            P(None, None, "tensor"),
            P("tensor", None),
            P(),
            P(),
            P(None, "tensor"),
            P("tensor", None),
            P("dp", "tensor", None),
        ),
        out_specs=(
            P("dp", "tensor", None),
            P("dp", "tensor", None),
            P(),
            P(),
            P(None, None, "tensor"),
            P("tensor", None),
            P(),
            P(),
            P(None, "tensor"),
            P("tensor", None),
        ),
        check_vma=False,
    )
```

profile of v0, /device:TPU:0, one launch (start us, length us, event | category | flops | bytes accessed | tf_op | source)
XLA Modules:
  0.0 1048.9 jit_solution(10486515235200515874)
XLA Ops:
  15.9 80.9 %all-gather.6.cloned.1.call-done = bf16[2048,1024]{1,0:T(8,128)(2,1)} async-done(((bf16[512,1024]{1,0:T(8,128)(2,1)}), bf16[2048,1024]{1,0:T(8,128)(2,1)}) %all-gather.6.cloned.1.call-update) | async-done | bytes 4194320 | tf_op jit(solution)/shard_map/all_gather | solution.py:75
  96.8 6.2 convolution_convert_fusion.4
  112.6 47.7 %while.30 = (s32[]{:T(128)}, bf16[4,512,256]{2,1,0:T(8,128)(2,1)}, f32[4,2,512]{2,1,0:T(2,128)S(1)}, s32[4]{0:T(128)S(1)}, bf16[2176,256]{0,1:T(8,128)(2,1)}, /*...) while((s32[]{:T(128)}, bf16[4,512,256]{2,1,0:T(8,128)(2,1)}, ...), condition=%wide.region_5.6_spmd, body=%wide.region_2.5_spmd.sunk | while | flops 344522240 | bytes 13289242 | solution.py:103
  160.3 4.5 convolution_convert_fusion.2
  164.8 75.4 %reduce-scatter.5.cloned.1.call-done = bf16[512,1024]{1,0:T(8,128)(2,1)} async-done(((bf16[2048,1024]{1,0:T(8,128)(2,1)}), bf16[512,1024]{1,0:T(8,128)(2,1)}) %reduce-scatter.5.cloned.1.call-update) | async-done | bytes 1048592 | tf_op jit(solution)/shard_map/reduce_scatter | solution.py:105
  244.8 80.6 %all-gather.8.cloned.1.call-done = bf16[2048,1024]{1,0:T(8,128)(2,1)} async-done(((bf16[512,1024]{1,0:T(8,128)(2,1)}), bf16[2048,1024]{1,0:T(8,128)(2,1)}) %all-gather.8.cloned.1.call-update) | async-done | bytes 4194320 | tf_op jit(solution)/shard_map/all_gather | solution.py:112
  325.3 14.7 %multiply_convert_fusion.1 = (bf16[2048,512]{1,0:T(8,128)(2,1)}, f32[2048,512]{1,0:T(8,128)}, f32[2048,512]{1,0:T(8,128)}) fusion(bf16[2048,1024]{1,0:T(8,128)(2,1)} %all-gather.8.cloned.1.call-done, bf16[1024,512]{1,0:T(8,128)(2,1)S(1)} %copy-done), kind=kOutput, calls=%fused_computation.54 | convolution fusion | flops 2215641088 | bytes 15728640 | tf_op jit(solution)/shard_map/dot_general | solution.py:113
  340.0 66.0 %all-gather.12.cloned.1.call-done = bf16[1,2048,1024]{2,1,0:T(8,128)(2,1)} async-done(((bf16[1,512,1024]{2,1,0:T(8,128)(2,1)}), bf16[1,2048,1024]{2,1,0:T(8,128)(2,1)}) %all-gather.12.cloned.1.call-update) | async-done | bytes 4194320 | tf_op jit(solution)/shard_map/all_gather | solution.py:123
  406.0 8.7 add_convert_fusion
  416.1 4.3 convolution_convert_fusion
  420.9 75.0 %reduce-scatter.9.cloned.1.call-done = bf16[512,1024]{1,0:T(8,128)(2,1)} async-done(((bf16[2048,1024]{1,0:T(8,128)(2,1)}), bf16[512,1024]{1,0:T(8,128)(2,1)}) %reduce-scatter.9.cloned.1.call-update) | async-done | bytes 1048592 | tf_op jit(solution)/shard_map/reduce_scatter | solution.py:129
  500.4 81.3 %all-gather.10.cloned.1.call-done = bf16[2048,1024]{1,0:T(8,128)(2,1)} async-done(((bf16[512,1024]{1,0:T(8,128)(2,1)}), bf16[2048,1024]{1,0:T(8,128)(2,1)}) %all-gather.10.cloned.1.call-update) | async-done | bytes 4194320 | tf_op jit(solution)/shard_map/all_gather | solution.py:139
  581.8 4.6 convolution_convert_fusion.5
  589.4 146.9 %while.31 = (s32[]{:T(128)}, f32[2176,256]{1,0:T(8,128)}, f32[2176,256]{1,0:T(8,128)}, bf16[4,512,256]{2,1,0:T(8,128)(2,1)}, s32[4]{0:T(128)S(1)}, /*index=5*/bf...) while((s32[]{:T(128)}, f32[2176,256]{1,0:T(8,128)}, ...), condition=%wide.region_15.16_spmd, body=%wide.region_13.15_spmd.sunk | while | flops 849350400 | bytes 53835736 | solution.py:186
  610.2 5.7 fusion.147
  615.9 5.8 fusion.146
  646.9 5.7 fusion.147
  652.6 5.8 fusion.146
  683.7 5.7 fusion.147
  689.3 5.8 fusion.146
  720.4 5.7 fusion.147
  726.1 5.8 fusion.146
  739.8 4.9 convolution_convert_fusion.3
  745.0 6.2 convolution_convert_fusion.1
  751.2 6.7 fusion.27
  761.6 5.2 fusion.65
  770.5 4.4 fusion.72
  775.0 45.2 %reduce-scatter.11.cloned.1.call-done = bf16[512,1024]{1,0:T(8,128)(2,1)} async-done(((bf16[2048,1024]{1,0:T(8,128)(2,1)}), bf16[512,1024]{1,0:T(8,128)(2,1)}) %reduce-scatter.11.cloned.1.call-update) | async-done | bytes 1048592 | tf_op jit(solution)/shard_map/reduce_scatter | solution.py:200
  822.4 46.2 %all-reduce.2 = (f32[1024]{0:T(1024)}, f32[1024]{0:T(1024)}, f32[1024]{0:T(1024)}, f32[1024]{0:T(1024)}) all-reduce(f32[1024]{0:T(1024)S(1)} %get-tuple-element.285, f32[1024]{0:T(1024)S(1)} %get-tuple-element.290, f32[1024]{0:T(1024)S(1)} %get-tuple-element.283, ...), channel_id=1, replica_groups=mesh['dp'=8,'tensor'=4] {'dp','tensor'}, use_global_device_ids=true, to_apply=%region_20.21 | all-reduce | flops 4096 | bytes 32768 | tf_op jit(solution)/shard_map/psum | solution.py:210
  868.6 32.2 %reduce-scatter.7.cloned.1.call-done = bf16[512,1024]{1,0:T(8,128)(2,1)} async-done(((bf16[2048,1024]{1,0:T(8,128)(2,1)}), bf16[512,1024]{1,0:T(8,128)(2,1)}) %reduce-scatter.7.cloned.1.call-update) | async-done | bytes 1048592 | tf_op jit(solution)/shard_map/reduce_scatter | solution.py:115
  900.9 4.4 fusion.55
  905.3 127.4 %all-reduce.6.cloned.1.call-done = (f32[1024,3,256]{2,0,1:T(8,128)}, f32[256,1024]{1,0:T(8,128)}, f32[1024,512]{1,0:T(8,128)}, f32[512,1024]{1,0:T(8,128)}) async-done(((f32[1024,3,256]{2,0,1:T(8,128)}, f32[256,1024]{1,0:T(8,128)}, f32[1024,512]{1,0:T(8,128)}, f32[512,1024]{1,0:T(8,128)}), (f32[1024,3,256]{2,0,1:T(8,128)}, f32[256,1024]{1,0:T(8,128)}, f32[1024,512]{1,0:T(8,128)}, ...) | async-done | bytes 8388624 | tf_op jit(solution)/shard_map/psum | solution.py:213
  (289 shorter events, 174.5 us)
Async XLA Ops:
  7.2 318.2 %copy-start = (bf16[1024,512]{1,0:T(8,128)(2,1)S(1)}, bf16[1024,512]{1,0:T(8,128)(2,1)}, u32[]{:S(2)}) copy-start(bf16[1024,512]{1,0:T(8,128)(2,1)} %param.23) | copy-start | bytes 3145732
  7.2 3.9 copy-start.2
  7.2 89.6 %all-gather.6.cloned.1.call-start = ((), (), s32[]{:S(2)}) async-start(), calls=%async_computation.4 | async-start | bytes 5242880 | tf_op jit(solution)/shard_map/all_gather | solution.py:75
  13.2 227.0 %reduce-scatter.5.cloned.1.call-start = ((), (), s32[]{:S(2)}) async-start(), calls=%async_computation.5 | async-start | bytes 5242880 | tf_op jit(solution)/shard_map/reduce_scatter | solution.py:105
  112.6 47.7 %copy-start.19 = (bf16[256,1024]{1,0:T(8,128)(2,1)S(1)}, bf16[256,1024]{1,0:T(8,128)(2,1)}, u32[]{:S(2)}) copy-start(bf16[256,1024]{1,0:T(8,128)(2,1)} %param.20) | copy-start | bytes 1572868
  164.8 77.6 %copy-start.20 = (f32[1024]{0:T(1024)S(1)}, f32[1024]{0:T(1024)}, u32[]{:S(2)}) copy-start(f32[1024]{0:T(1024)} %param.21) | copy-start | bytes 12292
  164.8 77.6 %copy-start.27 = (f32[1024]{0:T(1024)S(1)}, f32[1024]{0:T(1024)}, u32[]{:S(2)}) copy-start(f32[1024]{0:T(1024)} %param.22) | copy-start | bytes 12292
  164.8 160.5 %all-gather.8.cloned.1.call-start = ((), (), s32[]{:S(2)}) async-start(), calls=%async_computation.6 | async-start | bytes 5242880 | tf_op jit(solution)/shard_map/all_gather | solution.py:112
  243.9 162.1 %all-gather.12.cloned.1.call-start = ((), (), s32[]{:S(2)}) async-start(), calls=%async_computation.11 | async-start | bytes 5242880 | tf_op jit(solution)/shard_map/all_gather | solution.py:123
  244.5 251.3 %reduce-scatter.9.cloned.1.call-start = ((), (), s32[]{:S(2)}) async-start(), calls=%async_computation.8 | async-start | bytes 5242880 | tf_op jit(solution)/shard_map/reduce_scatter | solution.py:129
  420.4 77.9 %copy-start.6 = (bf16[1,512,1024]{2,1,0:T(8,128)(2,1)S(1)}, bf16[1,512,1024]{2,1,0:T(8,128)(2,1)}, u32[]{:S(2)}) copy-start(bf16[1,512,1024]{2,1,0:T(8,128)(2,1)} %param.25) | copy-start | bytes 3145732
  420.4 161.3 %all-gather.10.cloned.1.call-start = ((), (), s32[]{:S(2)}) async-start(), calls=%async_computation.9 | async-start | bytes 5242880 | tf_op jit(solution)/shard_map/all_gather | solution.py:139
  500.4 319.8 %reduce-scatter.11.cloned.1.call-start = ((), (), s32[]{:S(2)}) async-start(), calls=%async_computation.10 | async-start | bytes 5242880 | tf_op jit(solution)/shard_map/reduce_scatter | solution.py:200
  607.1 8.8 copy-start.10
  643.8 8.8 copy-start.10
  680.5 8.8 copy-start.10
  717.3 8.8 copy-start.10
  736.2 3.6 copy-start.29
  744.7 156.1 %reduce-scatter.7.cloned.1.call-start = ((), (), s32[]{:S(2)}) async-start(), calls=%async_computation.7 | async-start | bytes 5242880 | tf_op jit(solution)/shard_map/reduce_scatter | solution.py:115
  751.2 281.6 %all-reduce.6.cloned.1.call-start = ((), (), s32[]{:S(2)}) async-start(), calls=%async_computation.12 | async-start | bytes 16777216 | tf_op jit(solution)/shard_map/psum | solution.py:213
  751.2 6.7 copy-start.11
  751.2 6.7 copy-start.16
  757.9 3.7 copy-start.28
  757.9 3.7 copy-start.30
  766.9 3.6 copy-start.12
  774.9 45.3 %copy-start.22 = (f32[512]{0:T(512)S(1)}, f32[512]{0:T(512)}, u32[]{:S(2)}) copy-start(f32[512]{0:T(512)} %copy-done.21) | copy-start | bytes 6148
  774.9 45.3 %copy-start.23 = (f32[1024]{0:T(1024)S(1)}, f32[1024]{0:T(1024)}, u32[]{:S(2)}) copy-start(f32[1024]{0:T(1024)} %param.17) | copy-start | bytes 12292
  774.9 45.3 %copy-start.25 = (f32[512]{0:T(512)S(1)}, f32[512]{0:T(512)}, u32[]{:S(2)}) copy-start(f32[512]{0:T(512)} %copy-done.24) | copy-start | bytes 6148
  775.0 125.9 %copy-start.5 = (bf16[512,1024]{1,0:T(8,128)(2,1)S(1)}, bf16[512,1024]{1,0:T(8,128)(2,1)}, u32[]{:S(2)}) copy-start(bf16[512,1024]{1,0:T(8,128)(2,1)} %reduce-scatter.5.cloned.1.call-done) | copy-start | bytes 3145732
  775.0 125.9 %copy-start.7 = (bf16[1,512,1024]{2,1,0:T(8,128)(2,1)S(1)}, bf16[1,512,1024]{2,1,0:T(8,128)(2,1)}, u32[]{:S(2)}) copy-start(bf16[1,512,1024]{2,1,0:T(8,128)(2,1)} %param.25) | copy-start | bytes 3145732
  1032.7 3.8 copy-start.18
  1038.5 3.7 copy-start.1
  (17 other events, 36.7 us)
Sparse Core Ops, SparseCore 0:
  13.3 83.4 all-gather.5
  164.9 75.2 reduce-scatter.4
  244.1 81.2 all-gather.7
  326.8 79.2 all-gather.11
  420.5 75.2 reduce-scatter.8
  500.5 81.2 all-gather.9
  744.9 75.2 reduce-scatter.10
  822.5 78.3 reduce-scatter.6
  905.9 126.7 all-reduce.5
where the time goes:
time: 1060 us; the launch traced here: 1050 us
  waiting for transfers between devices  665 us (63%)
  matrix products  150 us (14%)
  local copies, waits for them, and re-layouts  109 us (10%)
  blocking collectives  46.2 us (4%)
  other arithmetic  34 us (3%)
  loops' own time  29.1 us (3%)
  between operations  14.3 us (1%)
    psum x1, waiting for transfers between devices, local(): lax.psum((grad_qkv, grad_wout, grad_win, grad_wdown), 'dp')  127 us
    all_gather x1, waiting for transfers between devices, local(): lax.all_gather(grad_mixed.astype(jnp.bfloat16), 'tensor', axis=0, tiled=T...  81.3 us
    all_gather x1, waiting for transfers between devices, local(): lax.all_gather(normed1.astype(jnp.bfloat16), 'tensor', axis=0, tiled=True)  80.9 us
    all_gather x1, waiting for transfers between devices, local(): lax.all_gather(normed2.astype(jnp.bfloat16), 'tensor', axis=0, tiled=True)  80.6 us
    reduce_scatter x1, waiting for transfers between devices, local(): lax.psum_scatter(jnp.dot(attended, w_out, preferred_element_type=jnp.floa...  75.4 us
    reduce_scatter x1, waiting for transfers between devices, local(): lax.psum_scatter(jnp.einsum('tf,df->td', grad_pre, w_in, preferred_elemen...  75 us
    all_gather x1, waiting for transfers between devices, local(): grad_full = lax.all_gather(cotangent[0], 'tensor', axis=0, tiled=True)  66 us
    psum x1, blocking collectives, local(): lax.psum((grad_gain1, grad_bias1, grad_gain2, grad_bias2), ('dp', 'tensor'))  46.2 us
  transfers between devices with their start and end apart: 9, of which 9 were waited for; matrix products, arithmetic and copies ran while one was open for 5% of the time, Pallas kernels for 0%

commit v1 on v0

v1 whole, which is shorter than its diff:
```python
import math

import jax
import jax.numpy as jnp
from jax import lax
from jax.sharding import PartitionSpec as P

HEAD_DIM = 128
eps_norm = 1e-05
halo = 16
query_block = 128
ALL = ("dp", "tensor")


def norm_forward(values, gain, bias):
    center = values - jnp.mean(values, axis=-1, keepdims=True)
    spread = jnp.mean(center * center, axis=-1, keepdims=True)
    scaled = lax.rsqrt(spread + eps_norm)
    normal = center * scaled
    return (normal * gain + bias, normal, scaled)


def norm_backward(upstream, normal, scaled, gain):
    weighted = upstream * gain
    inner = (
        weighted
        - jnp.mean(weighted, axis=-1, keepdims=True)
        - normal * jnp.mean(weighted * normal, axis=-1, keepdims=True)
    )
    return (scaled * inner, jnp.sum(upstream * normal, axis=0), jnp.sum(upstream, axis=0))


def gather_groups(shard):
    n_dp = lax.axis_size("dp")
    n_t = lax.axis_size("tensor")
    d = lax.axis_index("dp")
    rows = shard.shape[0] // n_dp
    piece = lax.dynamic_slice_in_dim(shard, d * rows, rows, 0)
    whole = lax.all_gather(piece, ALL, axis=0, tiled=False)
    whole = whole.reshape((n_dp, n_t) + piece.shape)
    whole = jnp.moveaxis(whole, 1, 0)
    return whole.reshape((n_t,) + shard.shape)


def reduce_groups(partial, extra=None):
    n_dp = lax.axis_size("dp")
    n_t, a, b = partial.shape
    pieces = partial.astype(jnp.bfloat16).reshape(n_t, n_dp, a // n_dp, b)
    if extra is not None:
        pieces = jnp.concatenate([pieces, extra.astype(jnp.bfloat16)], axis=2)
    part = lax.psum_scatter(pieces, "dp", scatter_dimension=1, tiled=True)
    part = lax.psum_scatter(part, "tensor", scatter_dimension=0, tiled=True)
    whole = lax.all_gather(part, "dp", axis=1, tiled=True)
    whole = whole.reshape(n_dp, whole.shape[2], b).astype(jnp.float32)
    if extra is None:
        return whole.reshape(a, b), None
    return whole[:, : a // n_dp].reshape(a, b), whole[0, a // n_dp :]


def local(
    tokens,
    seg_ids,
    norm1_gain,
    norm1_bias,
    w_qkv,
    w_out,
    norm2_gain,
    norm2_bias,
    w_in,
    w_down,
    cotangent,
):
    n_t = lax.axis_size("tensor")
    n_dp = lax.axis_size("dp")
    t = lax.axis_index("tensor")
    rows_here = tokens.shape[1]
    width = tokens.shape[2]
    cols = w_qkv.shape[2]
    heads_group = cols // HEAD_DIM
    units = w_in.shape[1]
    scale = HEAD_DIM ** (-0.5)
    nb = rows_here // query_block
    front = query_block - halo
    ext = rows_here + halo

    wqkv_all = gather_groups(w_qkv).reshape(n_t, width, 3 * cols)
    wout_all = gather_groups(w_out)
    win_all = gather_groups(jnp.swapaxes(w_in, 0, 1))
    wdown_all = gather_groups(w_down)

    own = tokens[0]
    prev = lax.ppermute(own[rows_here - halo :], "tensor", [(i, i + 1) for i in range(n_t - 1)])
    rows_ext = jnp.concatenate([prev, own], axis=0).astype(jnp.float32)
    normed1_f, normal1, rstd1 = norm_forward(rows_ext, norm1_gain, norm1_bias)
    normed1 = normed1_f.astype(jnp.bfloat16)

    seg_pack = seg_ids[0]
    seg_pad = jnp.concatenate([jnp.full((query_block,), -1, jnp.int32), seg_pack])
    seg_win = lax.dynamic_slice_in_dim(seg_pad, t * rows_here, rows_here + query_block, 0)
    seg_win = jnp.where(jnp.arange(rows_here + query_block) < front, -1, seg_win)
    seg_blocks = seg_win.reshape(nb + 1, query_block)
    query_segs = seg_blocks[1:]
    key_segs = jnp.concatenate([seg_blocks[:-1], seg_blocks[1:]], axis=1)
    causal = jnp.arange(2 * query_block)[None, :] <= (jnp.arange(query_block)[:, None] + query_block)
    allowed = (query_segs[:, :, None] == key_segs[:, None, :]) & causal[None]

    packed = jnp.einsum("rk,gkn->grn", normed1, wqkv_all, preferred_element_type=jnp.float32)
    packed = packed.astype(jnp.bfloat16)
    queries = packed[:, halo:, :cols].reshape(n_t, nb, query_block, heads_group, HEAD_DIM)

    def windows(part):
        padded = jnp.concatenate([jnp.zeros((n_t, front, cols), jnp.bfloat16), part], axis=1)
        blocks = padded.reshape(n_t, nb + 1, query_block, heads_group, HEAD_DIM)
        return jnp.concatenate([blocks[:, :-1], blocks[:, 1:]], axis=2)

    key_win = windows(packed[:, :, cols : 2 * cols])
    value_win = windows(packed[:, :, 2 * cols :])

    raw = jnp.einsum("gbqhd,gbkhd->gbhqk", queries, key_win, preferred_element_type=jnp.float32)
    masked = jnp.where(allowed[None, :, None], raw * scale, -1e30)
    top = jnp.max(masked, axis=-1, keepdims=True)
    expo = jnp.exp(masked - top)
    probs = expo / jnp.sum(expo, axis=-1, keepdims=True)
    probs_low = probs.astype(jnp.bfloat16)
    attended = jnp.einsum(
        "gbhqk,gbkhd->gbqhd", probs_low, value_win, preferred_element_type=jnp.float32
    ).astype(jnp.bfloat16)
    attended = attended.reshape(n_t, rows_here, cols)

    rows = rows_ext[halo:]
    mixed = rows + jnp.einsum("grc,gcn->rn", attended, wout_all, preferred_element_type=jnp.float32)
    normed2_f, normal2, rstd2 = norm_forward(mixed, norm2_gain, norm2_bias)
    normed2 = normed2_f.astype(jnp.bfloat16)
    pre_act = jnp.einsum("rk,guk->gru", normed2, win_all, preferred_element_type=jnp.float32)
    hidden = jax.nn.gelu(pre_act, approximate=False).astype(jnp.bfloat16)
    final = mixed + jnp.einsum("gru,gun->rn", hidden, wdown_all, preferred_element_type=jnp.float32)
    out_act = final.astype(jnp.bfloat16)[None]

    grad_low = cotangent[0]
    grad_wdown_part = jnp.einsum("gru,rn->gun", hidden, grad_low, preferred_element_type=jnp.float32)
    grad_hidden = jnp.einsum("rn,gun->gru", grad_low, wdown_all, preferred_element_type=jnp.float32)
    cdf = 0.5 * (1.0 + lax.erf(pre_act * (1.0 / math.sqrt(2.0))))
    pdf = jnp.exp(-0.5 * pre_act * pre_act) * (1.0 / math.sqrt(2.0 * math.pi))
    grad_pre = (grad_hidden * (cdf + pre_act * pdf)).astype(jnp.bfloat16)
    grad_win_part = jnp.einsum("rk,gru->guk", normed2, grad_pre, preferred_element_type=jnp.float32)
    grad_normed2 = jnp.einsum("gru,guk->rk", grad_pre, win_all, preferred_element_type=jnp.float32)
    grad_back2, grad_gain2, grad_bias2 = norm_backward(grad_normed2, normal2, rstd2, norm2_gain)
    grad_mixed = grad_low.astype(jnp.float32) + grad_back2
    mixed_low = grad_mixed.astype(jnp.bfloat16)
    grad_wout_part = jnp.einsum("grc,rn->gcn", attended, mixed_low, preferred_element_type=jnp.float32)
    grad_att = jnp.einsum("rn,gcn->grc", mixed_low, wout_all, preferred_element_type=jnp.float32)
    grad_att = grad_att.astype(jnp.bfloat16).reshape(n_t, nb, query_block, heads_group, HEAD_DIM)

    grad_prob = jnp.einsum("gbqhd,gbkhd->gbhqk", grad_att, value_win, preferred_element_type=jnp.float32)
    inner = jnp.sum(probs * grad_prob, axis=-1, keepdims=True)
    grad_raw = jnp.where(allowed[None, :, None], probs * (grad_prob - inner) * scale, 0.0)
    grad_raw = grad_raw.astype(jnp.bfloat16)
    grad_q = jnp.einsum("gbhqk,gbkhd->gbqhd", grad_raw, key_win, preferred_element_type=jnp.float32)
    grad_kw = jnp.einsum("gbhqk,gbqhd->gbkhd", grad_raw, queries, preferred_element_type=jnp.float32)
    grad_vw = jnp.einsum("gbhqk,gbqhd->gbkhd", probs_low, grad_att, preferred_element_type=jnp.float32)

    def unwindow(grad_w):
        first = jnp.pad(grad_w[:, :, :query_block], ((0, 0), (0, 1), (0, 0), (0, 0), (0, 0)))
        second = jnp.pad(grad_w[:, :, query_block:], ((0, 0), (1, 0), (0, 0), (0, 0), (0, 0)))
        summed = (first + second).reshape(n_t, (nb + 1) * query_block, cols)
        return summed[:, front:]

    grad_q = jnp.concatenate(
        [jnp.zeros((n_t, halo, cols), jnp.float32), grad_q.reshape(n_t, rows_here, cols)], axis=1
    )
    grad_proj = jnp.concatenate([grad_q, unwindow(grad_kw), unwindow(grad_vw)], axis=2)
    grad_proj = grad_proj.astype(jnp.bfloat16)
    grad_qkv_part = jnp.einsum("rk,grn->gkn", normed1, grad_proj, preferred_element_type=jnp.float32)
    grad_normed1 = jnp.einsum("grn,gkn->rk", grad_proj, wqkv_all, preferred_element_type=jnp.float32)
    back = lax.ppermute(grad_normed1[:halo], "tensor", [(i + 1, i) for i in range(n_t - 1)])
    grad_normed1 = grad_normed1[halo:] + jnp.pad(back, ((rows_here - halo, 0), (0, 0)))
    grad_back1, grad_gain1, grad_bias1 = norm_backward(
        grad_normed1, normal1[halo:], rstd1[halo:], norm1_gain
    )
    grad_tokens = (grad_mixed + grad_back1)[None]

    norm_total = lax.psum(jnp.stack([grad_gain1, grad_bias1, grad_gain2, grad_bias2]), ALL)
    grad_wdown, _ = reduce_groups(grad_wdown_part)
    grad_win, _ = reduce_groups(grad_win_part)
    grad_wout, _ = reduce_groups(grad_wout_part)
    grad_qkv, _ = reduce_groups(grad_qkv_part)
    return (
        out_act,
        grad_tokens,
        norm_total[0],
        norm_total[1],
        grad_qkv.reshape(width, 3, cols),
        grad_wout,
        norm_total[2],
        norm_total[3],
        jnp.swapaxes(grad_win, 0, 1),
        grad_wdown,
    )


def solution(mesh):
    return jax.shard_map(
        local,
        mesh=mesh,
        in_specs=(
            P("dp", "tensor", None),
            P("dp", None),
            P(),
            P(),
            P(None, None, "tensor"),
            P("tensor", None),
            P(),
            P(),
            P(None, "tensor"),
            P("tensor", None),
            P("dp", "tensor", None),
        ),
        out_specs=(
            P("dp", "tensor", None),
            P("dp", "tensor", None),
            P(),
            P(),
            P(None, None, "tensor"),
            P("tensor", None),
            P(),
            P(),
            P(None, "tensor"),
            P("tensor", None),
        ),
        check_vma=False,
    )
```

time: 1060 us -> 784 us (0.74)
  waiting for transfers between devices: 665 us -> 413 us
  loops' own time: 29.1 us -> 0 us
  local copies, waits for them, and re-layouts: 109 us -> 137 us
  other arithmetic: 34 us -> 20.4 us
  matrix products: 150 us -> 137 us
    psum x1 -> x0, waiting for transfers between devices: 127 us -> none  [local(): lax.psum((grad_qkv, grad_wout, grad_win, grad_wdown), 'dp')]
    reduce_scatter x4 -> x5, waiting for transfers between devices: 228 us -> 119 us  [the longest x1 59.9 us: reduce_groups(): part = lax.psum_scatter(pieces, 'dp', scatter_dimension=1, tiled=True)]
    dynamic_slice x68 -> x3, local copies, waits for them, and re-layouts: 52.2 us -> 3.9 us  [gather_groups(): piece = lax.dynamic_slice_in_dim(shard, d * rows, rows, 0)]
    all_gather x4 -> x7, waiting for transfers between devices: 309 us -> 261 us  [the longest x4 235 us: gather_groups(): whole = lax.all_gather(piece, ALL, axis=0, tiled=False)]
    reshape x1 -> x13, local copies, waits for them, and re-layouts: 3.63 us -> 49.5 us  [the longest x3 17.3 us: gather_groups(): whole = whole.reshape((n_dp, n_t) + piece.shape)]
    unnamed x9 -> x14, waiting for transfers between devices: 0.65 us -> 31.2 us
    another operation x2 -> x0, loops' own time: 29.1 us -> none  [the longest x1 18.3 us: local(): blocks_out, log_mass = lax.map(attend, jnp.arange(nblocks) * block)]
    dot_general x40 -> x17, matrix products: 150 us -> 132 us  [the longest x1 28.6 us: local(): jnp.einsum('gbhqk,gbkhd->gbqhd', grad_raw, key_win, preferred_element_typ...]
  transfers between devices with their start and end apart: 9 -> 15, of which waited for: 9 -> 12; matrix products, arithmetic and copies ran while one was open for 5% -> 22% of each run, Pallas kernels for 0% -> 0%
where the time goes in v1:
time: 784 us; the launch traced here: 779 us
  waiting for transfers between devices  413 us (53%)
  local copies, waits for them, and re-layouts  137 us (17%)
  matrix products  137 us (17%)
  blocking collectives  50.2 us (6%)
  other arithmetic  20.4 us (3%)
  between operations  14.9 us (2%)
    all_gather x4, waiting for transfers between devices, gather_groups(): whole = lax.all_gather(piece, ALL, axis=0, tiled=False)  235 us
    reduce_scatter x1, waiting for transfers between devices, reduce_groups(): part = lax.psum_scatter(pieces, 'dp', scatter_dimension=1, tiled=True)  59.9 us
    reduce_scatter x4, waiting for transfers between devices, reduce_groups(): part = lax.psum_scatter(part, 'tensor', scatter_dimension=0, tiled=True)  58.9 us
    psum x1, blocking collectives, local(): lax.psum(jnp.stack([grad_gain1, grad_bias1, grad_gain2, grad_bias2]), ALL)  38.7 us
    unnamed x14, waiting for transfers between devices  31.2 us
    unnamed x65, local copies, waits for them, and re-layouts  30.1 us
    dot_general x1, matrix products, local(): jnp.einsum('gbhqk,gbkhd->gbqhd', grad_raw, key_win, preferred_element_typ...  28.6 us
    dot_general x1, matrix products, local(): jnp.einsum('gbhqk,gbqhd->gbkhd', grad_raw, queries, preferred_element_typ...  27.3 us
  transfers between devices with their start and end apart: 15, of which 12 were waited for; matrix products, arithmetic and copies ran while one was open for 22% of the time, Pallas kernels for 0%

profile of v1, /device:TPU:0, one launch (start us, length us, event | category | flops | bytes accessed | tf_op | source)
XLA Modules:
  0.0 779.1 jit_solution(15995433903944310363)
XLA Ops:
  13.4 5.0 collective-permute-start
  22.2 48.4 %all-gather.20.cloned.1.call-done = bf16[1024,1024]{1,0:T(8,128)(2,1)} async-done(((bf16[32,1024]{1,0:T(8,128)(2,1)}), bf16[1024,1024]{1,0:T(8,128)(2,1)}) %all-gather.20.cloned.1.call-update) | async-done | bytes 2097168 | tf_op jit(solution)/shard_map/all_gather | solution.py:39
  73.8 60.9 %all-gather.22.cloned.1.call-done = bf16[2048,1024]{1,0:T(8,128)(2,1)} async-done(((bf16[64,1024]{1,0:T(8,128)(2,1)}), bf16[2048,1024]{1,0:T(8,128)(2,1)}) %all-gather.22.cloned.1.call-update) | async-done | bytes 4194320 | tf_op jit(solution)/shard_map/all_gather | solution.py:39
  134.7 4.8 copy.75
  139.6 59.2 %all-gather.24.cloned.1.call-done = bf16[2048,1024]{1,0:T(8,128)(2,1)} async-done(((bf16[64,1024]{1,0:T(8,128)(2,1)}), bf16[2048,1024]{1,0:T(8,128)(2,1)}) %all-gather.24.cloned.1.call-update) | async-done | bytes 4194320 | tf_op jit(solution)/shard_map/all_gather | solution.py:39
  198.8 4.9 copy.76
  203.7 66.6 %all-gather.18.cloned.1.call-done = bf16[4096,3,256]{2,0,1:T(8,128)(2,1)} async-done(((bf16[128,3,256]{2,0,1:T(8,128)(2,1)}), bf16[4096,3,256]{2,0,1:T(8,128)(2,1)}) %all-gather.18.cloned.1.call-update) | async-done | bytes 6291472 | tf_op jit(solution)/shard_map/all_gather | solution.py:39
  270.3 9.2 %copy.65 = bf16[8,4,128,3,256]{2,0,4,3,1:T(8,128)(2,1)} copy(bf16[8,4,128,3,256]{4,2,1,0,3:T(8,128)(2,1)} %bitcast.227) | data formatting | bytes 12582912 | tf_op jit(solution)/shard_map/reshape | solution.py:40
  279.5 10.4 %reshape_reshape.4 = bf16[4,1024,768]{1,2,0:T(8,128)(2,1)} reshape(bf16[4,8,128,3,256]{2,1,4,3,0:T(8,128)(2,1)} %bitcast.217) | data formatting | bytes 12582912 | tf_op jit(solution)/shard_map/reshape;reshape | solution.py:86
  289.9 7.0 convert_bitcast_fusion
  325.4 5.6 fusion.101
  346.4 11.2 %fusion.5 = (bf16[4,512,512]{1,2,0:T(8,128)(2,1)S(1)}, f32[4,512,512]{2,1,0:T(8,128)S(1)}) fusion(bf16[4,512,1024]{2,1,0:T(8,128)(2,1)S(1)} %bitcast.233, f32[512,1024]{1,0:T(8,128)S(1)} %get-tuple-element.60, f32[1024]{0:T(1024)S(1)} %copy-done.24, f32[1024]{0:T(1024)S(1)} %copy-done.23, f32[512]{0:T(512)S(1)} %add_rsqrt_fusion.1, ...), kind=kOutput, calls=%fused_computation.8 | convolution fusion | flops 2218262528 | bytes 12595200 | tf_op jit(solution)/shard_map/rk,guk->gru/dot_general | solution.py:134
  363.9 4.6 convolution_convert_fusion.2
  376.7 4.5 fusion.51
  383.6 4.4 fusion.56
  387.9 28.6 %fusion.52 = bf16[4,4,128,2,128]{2,4,3,1,0:T(8,128)(2,1)} fusion(bf16[4,4,256,2,128]{4,2,3,1,0:T(8,128)(2,1)} %copy_dynamic-update-slice_fusion, f32[4,4,2,128,256]{4,3,2,1,0:T(8,128)} %fusion.56, pred[4,128,256]{2,1,0:T(8,128)(4,1)S(1)} %compare_and_fusion, f32[4,4,2,128,256]{4,3,2,1,0:T(8,128)} %get-tuple-element.58, ...), kind=kOutput, calls=%fused_computation.94 | convolution fusion | flops 277352704 | bytes 11681792 | tf_op jit(solution)/shard_map/gbhqk,gbkhd->gbqhd/dot_general | solution.py:158
  435.1 27.3 %convolution_bitcast_fusion.1 = f32[4,4,256,2,128]{2,4,3,1,0:T(8,128)} fusion(bf16[4,4,128,2,128]{2,4,3,1,0:T(8,128)(2,1)S(1)} %copy-done.18, f32[4,4,2,128,256]{4,3,2,1,0:T(8,128)} %fusion.56, pred[4,128,256]{2,1,0:T(8,128)(4,1)S(1)} %compare_and_fusion, f32[4,4,2,128,256]{4,3,2,1,0:T(8,128)} %get-tuple-element.58, f32[4,4,2,128]{3,2,1,0:T(2,128)S(1)} %get-tuple-element.57), kind=kOutput, calls=%fused_computation.55 | convolution fusion | flops 276828416 | bytes 13778944 | tf_op jit(solution)/shard_map/gbhqk,gbqhd->gbkhd/dot_general | solution.py:159
  473.3 5.8 convolution_convert_fusion
  483.3 9.2 %copy.88 = bf16[4,8,128,768]{3,2,0,1:T(8,128)(2,1)} copy(bf16[4,8,128,768]{2,1,3,0:T(8,128)(2,1)} %bitcast.218) | data formatting | bytes 12582912 | tf_op jit(solution)/shard_map/reshape | solution.py:48
  493.8 31.0 %all-reduce.15.cloned.1.call-done = (bf16[4,8,32,1024]{3,2,1,0:T(8,128)(2,1)}, bf16[4,8,64,1024]{3,2,1,0:T(8,128)(2,1)}, bf16[4,8,64,1024]{3,2,1,0:T(8,128)(2,1)}) async-done(((bf16[4,8,32,1024]{3,2,1,0:T(8,128)(2,1)}, bf16[4,8,64,1024]{3,2,1,0:T(8,128)(2,1)}, bf16[4,8,64,1024]{3,2,1,0:T(8,128)(2,1)}), (bf16[4,8,32,1024]{3,2,1,0:T(8,128)(2,1)}, bf16[4,8,64,1024]{3,2,1,0:T(8,128)(2,1)}, ...) | async-done | bytes 10485776
  529.9 59.9 %reduce-scatter.15.cloned.1.call-done = bf16[4,1,128,768]{3,2,0,1:T(8,128)(2,1)} async-done(((bf16[4,8,128,768]{3,2,0,1:T(8,128)(2,1)}), bf16[4,1,128,768]{3,2,0,1:T(8,128)(2,1)}) %reduce-scatter.15.cloned.1.call-update) | async-done | bytes 786448 | tf_op jit(solution)/shard_map/reduce_scatter | solution.py:51
  592.3 22.2 %reduce-scatter.21.cloned.1.call-done = bf16[1,1,64,1024]{3,2,1,0:T(8,128)(2,1)} async-done(((bf16[4,1,64,1024]{3,2,1,0:T(8,128)(2,1)}), bf16[1,1,64,1024]{3,2,1,0:T(8,128)(2,1)}) %reduce-scatter.21.cloned.1.call-update) | async-done | bytes 131088 | tf_op jit(solution)/shard_map/reduce_scatter | solution.py:52
  614.6 22.9 %reduce-scatter.23.cloned.1.call-done = bf16[1,1,64,1024]{3,2,1,0:T(8,128)(2,1)} async-done(((bf16[4,1,64,1024]{3,2,1,0:T(8,128)(2,1)}), bf16[1,1,64,1024]{3,2,1,0:T(8,128)(2,1)}) %reduce-scatter.23.cloned.1.call-update) | async-done | bytes 131088 | tf_op jit(solution)/shard_map/reduce_scatter | solution.py:52
  639.3 7.0 convolution_bitcast_fusion.2
  648.9 13.8 %reduce-scatter.17.cloned.1.call-done = bf16[1,1,128,768]{3,2,1,0:T(8,128)(2,1)} async-done(((bf16[4,1,128,768]{3,2,1,0:T(8,128)(2,1)}), bf16[1,1,128,768]{3,2,1,0:T(8,128)(2,1)}) %reduce-scatter.17.cloned.1.call-update) | async-done | bytes 196624 | tf_op jit(solution)/shard_map/reduce_scatter | solution.py:52
  662.7 6.9 fusion.55
  670.4 38.7 %psum.7 = f32[4,1024]{1,0:T(4,128)S(1)} all-reduce(f32[4,1024]{1,0:T(4,128)S(1)} %pad_maximum_fusion.4), channel_id=1, replica_groups=mesh['dp'=8,'tensor'=4] {'dp','tensor'}, use_global_device_ids=true, to_apply=%region_15.16 | all-reduce | flops 4096 | bytes 32768 | tf_op jit(solution)/shard_map/psum | solution.py:182
  709.7 4.7 add_bitcast_fusion
  714.4 11.5 %all_gather.45 = bf16[1,8,32,1024]{3,2,0,1:T(8,128)(2,1)S(1)} all-gather(bf16[1,1,32,1024]{3,2,0,1:T(8,128)(2,1)} %bitcast.244), channel_id=1, replica_groups=mesh['dp'=8,'tensor'=4] {'dp'}, dimensions={1}, use_global_device_ids=true | all-gather | bytes 589824 | tf_op jit(solution)/shard_map/all_gather | solution.py:53
  737.2 24.7 %all-gather.12.cloned.1.call-done = bf16[1,8,128,768]{3,2,0,1:T(8,128)(2,1)} async-done(((bf16[1,1,128,768]{3,2,0,1:T(8,128)(2,1)}), bf16[1,8,128,768]{3,2,0,1:T(8,128)(2,1)}) %all-gather.12.cloned.1.call-update) | async-done | bytes 1572880 | tf_op jit(solution)/shard_map/all_gather | solution.py:53
  761.9 5.7 reshape.251
  767.6 4.5 copy.97
  (162 shorter events, 133.3 us)
Async XLA Ops:
  7.2 5.4 copy-start
  7.2 6.2 copy-start.4
  7.2 11.2 %copy-start.22 = (s32[1,2048]{1,0:T(1,128)S(1)}, s32[1,2048]{1,0:T(1,128)}, u32[]{:S(2)}) copy-start(s32[1,2048]{1,0:T(1,128)} %param.12) | copy-start | bytes 24580
  7.2 63.4 %all-gather.20.cloned.1.call-start = ((), (), s32[]{:S(2)}) async-start(), calls=%async_computation.14 | async-start | bytes 2162688 | tf_op jit(solution)/shard_map/all_gather | solution.py:39
  8.9 125.8 %all-gather.22.cloned.1.call-start = ((), (), s32[]{:S(2)}) async-start(), calls=%async_computation.15 | async-start | bytes 4325376 | tf_op jit(solution)/shard_map/all_gather | solution.py:39
  10.9 187.9 %all-gather.24.cloned.1.call-start = ((), (), s32[]{:S(2)}) async-start(), calls=%async_computation.16 | async-start | bytes 4325376 | tf_op jit(solution)/shard_map/all_gather | solution.py:39
  12.5 257.8 %all-gather.18.cloned.1.call-start = ((), (), s32[]{:S(2)}) async-start(), calls=%async_computation.13 | async-start | bytes 6488064 | tf_op jit(solution)/shard_map/all_gather | solution.py:39
  13.3 511.4 %all-reduce.15.cloned.1.call-start = ((), (), s32[]{:S(2)}) async-start(), calls=%async_computation.17 | async-start | bytes 20971520
  13.4 6.5 collective-permute-start
  279.5 10.4 %copy-start.21 = (f32[1024]{0:T(1024)S(1)}, f32[1024]{0:T(1024)}, u32[]{:S(2)}) copy-start(f32[1024]{0:T(1024)} %param.13) | copy-start | bytes 12292
  279.5 10.4 %copy-start.25 = (f32[1024]{0:T(1024)S(1)}, f32[1024]{0:T(1024)}, u32[]{:S(2)}) copy-start(f32[1024]{0:T(1024)} %param.14) | copy-start | bytes 12292
  311.4 5.9 copy-start.9
  325.4 5.6 copy-start.10
  341.9 4.4 copy-start.12
  346.0 22.6 %copy-start.2 = (f32[512,1024]{1,0:T(8,128)}, f32[512,1024]{1,0:T(8,128)S(1)}, u32[]{:S(2)}) copy-start(f32[512,1024]{1,0:T(8,128)S(1)} %get-tuple-element.60) | copy-start | bytes 6291460
  346.4 11.2 %copy-start.5 = (bf16[8,4,64,1024]{3,2,0,1:T(8,128)(2,1)S(1)}, bf16[8,4,64,1024]{3,2,0,1:T(8,128)(2,1)}, u32[]{:S(2)}) copy-start(bf16[8,4,64,1024]{3,2,0,1:T(8,128)(2,1)} %copy.76) | copy-start | bytes 12582916
  346.4 11.2 %copy-start.20 = (bf16[1,512,1024]{2,1,0:T(8,128)(2,1)S(1)}, bf16[1,512,1024]{2,1,0:T(8,128)(2,1)}, u32[]{:S(2)}) copy-start(bf16[1,512,1024]{2,1,0:T(8,128)(2,1)} %param.21) | copy-start | bytes 3145732
  357.6 14.8 %copy-start.14 = (bf16[4,512,512]{1,2,0:T(8,128)(2,1)}, bf16[4,512,512]{1,2,0:T(8,128)(2,1)S(1)}, u32[]{:S(2)}) copy-start(bf16[4,512,512]{1,2,0:T(8,128)(2,1)S(1)} %get-tuple-element.61) | copy-start | bytes 6291460
  376.7 213.1 %reduce-scatter.15.cloned.1.call-start = ((), (), s32[]{:S(2)}) async-start(), calls=%async_computation.5 | async-start | bytes 7077888 | tf_op jit(solution)/shard_map/reduce_scatter | solution.py:51
  416.5 6.3 copy-start.11
  473.3 5.8 copy-start.16
  492.6 122.0 %reduce-scatter.21.cloned.1.call-start = ((), (), s32[]{:S(2)}) async-start(), calls=%async_computation.9 | async-start | bytes 655360 | tf_op jit(solution)/shard_map/reduce_scatter | solution.py:52
  527.3 110.2 %reduce-scatter.23.cloned.1.call-start = ((), (), s32[]{:S(2)}) async-start(), calls=%async_computation.11 | async-start | bytes 655360 | tf_op jit(solution)/shard_map/reduce_scatter | solution.py:52
  529.9 132.8 %reduce-scatter.17.cloned.1.call-start = ((), (), s32[]{:S(2)}) async-start(), calls=%async_computation.6 | async-start | bytes 983040 | tf_op jit(solution)/shard_map/reduce_scatter | solution.py:52
  589.8 124.6 %reduce-scatter.19.cloned.1.call-start = ((), (), s32[]{:S(2)}) async-start(), calls=%async_computation.8 | async-start | bytes 327680 | tf_op jit(solution)/shard_map/reduce_scatter | solution.py:52
  592.3 134.8 %all-gather.14.cloned.1.call-start = ((), (), s32[]{:S(2)}) async-start(), calls=%async_computation.10 | async-start | bytes 1179648 | tf_op jit(solution)/shard_map/all_gather | solution.py:53
  614.5 119.9 %all-gather.16.cloned.1.call-start = ((), (), s32[]{:S(2)}) async-start(), calls=%async_computation.12 | async-start | bytes 1179648 | tf_op jit(solution)/shard_map/all_gather | solution.py:53
  637.5 124.4 %all-gather.12.cloned.1.call-start = ((), (), s32[]{:S(2)}) async-start(), calls=%async_computation.7 | async-start | bytes 1769472 | tf_op jit(solution)/shard_map/all_gather | solution.py:53
  647.6 22.0 %collective-permute-start.1 = (f32[16,1024]{1,0:T(8,128)S(1)}, f32[16,1024]{1,0:T(8,128)S(1)}, u32[]{:S(2)}, u32[]{:S(2)}) collective-permute-start(f32[16,1024]{1,0:T(8,128)S(1)} %slice.149), channel_id=1, source_target_pairs={{1,0},{2,1},{3,2},{5,4},{6,5},{7,6},{9,8},{10,9},{11,10},{13,12},{... | collective-permute-start | bytes 196616 | tf_op jit(solution)/shard_map/ppermute | solution.py:175
  662.7 7.0 copy-start.3
  662.7 6.9 copy-start.7
  761.9 10.2 %copy-start.1 = (bf16[1024,3,256]{2,0,1:T(8,128)(2,1)S(1)}, bf16[1024,3,256]{2,0,1:T(8,128)(2,1)}, u32[]{:S(2)}) copy-start(bf16[1024,3,256]{2,0,1:T(8,128)(2,1)} %param.15) | copy-start | bytes 4718596
  (10 other events, 24.3 us)
Sparse Core Ops, SparseCore 0:
  11.5 59.0 all-gather.19
  74.2 60.4 all-gather.21
  138.3 60.4 all-gather.23
  202.2 68.0 all-gather.17
  376.8 147.8 all-reduce.14
  528.0 61.8 reduce-scatter.14
  592.7 21.8 reduce-scatter.20
  617.4 20.1 reduce-scatter.22
  639.8 22.7 reduce-scatter.16
  664.8 19.4 reduce-scatter.18
  686.2 21.9 all-gather.13
  709.9 24.4 all-gather.15
  736.3 25.5 all-gather.11
